TPU v7x, 32 devices: a whole 2x2x4 slice. The times are simulated.
32 devices in a mesh: grad: 4 (over y, x), col: 8 (over z, core).
Axes of the slice: x: 2, y: 2, z: 4, core: 2. Of those that a mesh axis runs over, the one named last changes fastest.
Arguments:
- gradient: bfloat16 [16384, 53248], P(('grad', 'col'))
- test_matrix: bfloat16 [16384, 256], P(('grad', 'col')), may hold values from -6 to 6
Outputs:
- low_rank: float32 [16384, 256], P(('grad', 'col'))
- projector: float32 [53248, 256], P('col')
All inputs are finite; a program needn't handle non-finite values.
Results may differ from a plain program's by a relative error of at most 0.008.
Values may be sent and summed in bfloat16 or wider, within the bound.
No kernel may reach another device: no remote copies, remote signals or barrier semaphores. Data moves between devices by JAX's collectives and lax.ppermute only.
A program may use at most 256 MiB of HBM per device.

v0:
```python
import math
import jax
import jax.numpy as jnp
from jax import lax
from jax.sharding import PartitionSpec as P

FF = 53248
POWER = 2


def orthonormal(rows):
    partial_gram = lax.dot_general(
        rows,
        rows,
        (((0,), (0,)), ((), ())),
        precision=lax.Precision.HIGHEST,
        preferred_element_type=jnp.float32,
    )
    gram = lax.psum(partial_gram, ("grad", "col"))
    lower_factor = jnp.linalg.cholesky(gram)
    return lax.linalg.triangular_solve(
        lower_factor, rows, left_side=False, lower=True, transpose_a=True
    )


def shards(gradient, test_matrix):
    n_grad = lax.axis_size("grad")
    n_col = lax.axis_size("col")
    n_rows, n_ff = gradient.shape
    piece = n_ff // (n_col * n_grad)
    split = gradient.reshape(n_rows, n_col, n_grad, piece)
    blocks = lax.all_to_all(split, "grad", split_axis=2, concat_axis=0, tiled=True)
    blocks = blocks.reshape(n_grad * n_rows, n_col * piece)

    def sketch_of(row_piece):
        rows = lax.all_gather(row_piece, "grad", axis=0, tiled=True)
        partial = lax.dot_general(
            blocks, rows, (((0,), (0,)), ((), ())), preferred_element_type=jnp.float32
        )
        return lax.psum_scatter(partial, "col", scatter_dimension=0, tiled=True)

    sketch = sketch_of(test_matrix)
    for iteration in range(POWER + 1):
        basis_rows = orthonormal(sketch)
        basis_bf = lax.all_gather(basis_rows.astype(jnp.bfloat16), "col", axis=0, tiled=True)
        reduced = lax.psum_scatter(
            jnp.dot(blocks, basis_bf, preferred_element_type=jnp.float32),
            "grad",
            scatter_dimension=0,
            tiled=True,
        )
        if iteration < POWER:
            sketch = sketch_of(reduced.astype(jnp.bfloat16))
    projector = lax.all_gather(basis_rows * math.sqrt(FF), "grad", axis=0, tiled=True)
    return (reduced, projector)


def solution(mesh):
    return jax.shard_map(
        shards,
        mesh=mesh,
        in_specs=(P(("grad", "col"), None), P(("grad", "col"), None)),
        out_specs=(P(("grad", "col"), None), P("col", None)),
        check_vma=False,
    )
```

profile of v0, /device:TPU:0, one launch (start us, length us, event | category | flops | bytes accessed | tf_op | source)
XLA Modules:
  0.0 2358.2 jit_solution(13075918259095874959)
XLA Ops:
  7.2 73.2 %reshape.28 = bf16[512,8,4,1664]{3,2,1,0:T(4,128)(2,1)} reshape(bf16[512,53248]{1,0:T(8,128)(2,1)} %param.5) | data formatting | bytes 109051904 | tf_op jit(solution)/shard_map/reshape | solution.py:31
  80.4 36.6 %copy.12 = bf16[512,8,4,1664]{3,1,0,2:T(8,128)(2,1)} copy(bf16[512,8,4,1664]{3,2,1,0:T(4,128)(2,1)} %reshape.28) | data formatting | bytes 109051904 | tf_op jit(solution)/shard_map/reshape | solution.py:31
  117.0 12.1 all-to-all-start
  129.8 596.0 %all-to-all-done = bf16[512,8,4,1664]{3,1,0,2:T(8,128)(2,1)} async-done(((bf16[512,8,4,1664]{3,1,0,2:T(8,128)(2,1)}), bf16[512,8,4,1664]{3,1,0,2:T(8,128)(2,1)}, u32[]{:S(2)}, u32[]{:S(2)}) %all-to-all-start) | async-done | bytes 54525984 | tf_op jit(solution)/shard_map/all_to_all | solution.py:32
  725.8 36.6 %copy.24 = bf16[256,8,8,1664]{3,1,2,0:T(8,128)(2,1)} copy(bf16[256,8,8,1664]{3,2,1,0:T(8,128)(2,1)} %bitcast.37) | data formatting | bytes 109051904
  762.4 28.2 %fusion.37 = f32[13312,256]{1,0:T(8,128)} fusion(bf16[2048,13312]{1,0:T(8,128)(2,1)} %bitcast.131, bf16[2048,256]{1,0:T(8,128)(2,1)} %all-gather.8.cloned.1.call-done), kind=kOutput, calls=%fused_computation.90 | convolution fusion | flops 13958643712 | bytes 69206016 | tf_op jit(solution)/shard_map/dot_general | solution.py:37
  790.7 139.5 %reduce-scatter.7.cloned.1.call-done = f32[1664,256]{1,0:T(8,128)} async-done(((f32[13312,256]{1,0:T(8,128)}), f32[1664,256]{1,0:T(8,128)}) %reduce-scatter.7.cloned.1.call-update) | async-done | bytes 1703952 | tf_op jit(solution)/shard_map/reduce_scatter | solution.py:40
  930.2 5.9 fusion.38
  936.6 124.7 %all-reduce.5.cloned.1.call-done = f32[256,256]{0,1:T(8,128)} async-done(((f32[256,256]{0,1:T(8,128)}), f32[256,256]{0,1:T(8,128)}) %all-reduce.5.cloned.1.call-update) | async-done | bytes 262160 | tf_op jit(solution)/shard_map/psum | solution.py:19
  1061.3 1.1 copy.14
  1062.4 1.0 fusion.10
  1063.4 11.7 cholesky.172
  1075.2 9.8 custom-call.15
  1085.5 11.7 cholesky.189
  1099.3 4.1 while.6
  1100.1 1.4 bitcast_dynamic-update-slice_fusion.6
  1102.1 1.4 bitcast_dynamic-update-slice_fusion.6
  1103.5 19.7 custom-call.16
  1124.1 1.5 convolution_subtract_fusion.2
  1127.7 68.2 %all-gather.10.cloned.1.call-done = bf16[13312,256]{0,1:T(8,128)(2,1)} async-done(((bf16[1664,256]{0,1:T(8,128)(2,1)}), bf16[13312,256]{0,1:T(8,128)(2,1)}) %all-gather.10.cloned.1.call-update) | async-done | bytes 6815760 | tf_op jit(solution)/shard_map/all_gather | solution.py:45
  1195.9 24.2 %convolution_bitcast_fusion.4 = f32[2048,256]{0,1:T(8,128)} fusion(bf16[13312,256]{0,1:T(8,128)(2,1)} %all-gather.10.cloned.1.call-done, bf16[2048,13312]{1,0:T(8,128)(2,1)} %bitcast.132), kind=kOutput, calls=%fused_computation.10 | convolution fusion | flops 13958643712 | bytes 63438848 | tf_op jit(solution)/shard_map/dot_general | solution.py:47
  1220.2 33.9 %reduce-scatter.9.cloned.1.call-done = f32[512,256]{0,1:T(8,128)} async-done(((f32[2048,256]{0,1:T(8,128)}), f32[512,256]{0,1:T(8,128)}) %reduce-scatter.9.cloned.1.call-update) | async-done | bytes 524304 | tf_op jit(solution)/shard_map/reduce_scatter | solution.py:46
  1254.1 1.8 convert_element_type.16
  1255.9 26.8 %all-gather.12.cloned.1.call-done = bf16[2048,256]{0,1:T(8,128)(2,1)} async-done(((bf16[512,256]{0,1:T(8,128)(2,1)}), bf16[2048,256]{0,1:T(8,128)(2,1)}) %all-gather.12.cloned.1.call-update) | async-done | bytes 1048592 | tf_op jit(solution)/shard_map/all_gather | solution.py:36
  1282.7 28.3 %convolution_bitcast_fusion.1 = f32[13312,256]{0,1:T(8,128)} fusion(bf16[2048,256]{0,1:T(8,128)(2,1)} %all-gather.12.cloned.1.call-done, bf16[2048,13312]{1,0:T(8,128)(2,1)} %bitcast.133), kind=kOutput, calls=%fused_computation.7 | convolution fusion | flops 13958643712 | bytes 69206016 | tf_op jit(solution)/shard_map/dot_general | solution.py:37
  1311.3 138.9 %reduce-scatter.11.cloned.1.call-done = f32[1664,256]{0,1:T(8,128)} async-done(((f32[13312,256]{0,1:T(8,128)}), f32[1664,256]{0,1:T(8,128)}) %reduce-scatter.11.cloned.1.call-update) | async-done | bytes 1703952 | tf_op jit(solution)/shard_map/reduce_scatter | solution.py:40
  1450.3 4.7 fusion.39
  1455.0 126.4 %all-reduce.7.cloned.1.call-done = f32[256,256]{0,1:T(8,128)} async-done(((f32[256,256]{0,1:T(8,128)}), f32[256,256]{0,1:T(8,128)}) %all-reduce.7.cloned.1.call-update) | async-done | bytes 262160 | tf_op jit(solution)/shard_map/psum | solution.py:19
  1581.4 1.1 copy.16
  1582.5 1.0 fusion.9
  1583.5 11.7 cholesky.206
  1595.3 9.8 custom-call.17
  1605.6 11.7 cholesky.223
  1620.0 4.4 while.7
  1621.0 1.4 bitcast_dynamic-update-slice_fusion.7
  1623.0 1.4 bitcast_dynamic-update-slice_fusion.7
  1624.3 19.7 custom-call.18
  1646.7 1.0 maximum_convert_fusion.1
  1647.8 68.2 %all-gather.14.cloned.1.call-done = bf16[13312,256]{0,1:T(8,128)(2,1)} async-done(((bf16[1664,256]{0,1:T(8,128)(2,1)}), bf16[13312,256]{0,1:T(8,128)(2,1)}) %all-gather.14.cloned.1.call-update) | async-done | bytes 6815760 | tf_op jit(solution)/shard_map/all_gather | solution.py:45
  1716.0 24.3 %convolution_bitcast_fusion.3 = f32[2048,256]{0,1:T(8,128)} fusion(bf16[13312,256]{0,1:T(8,128)(2,1)} %all-gather.14.cloned.1.call-done, bf16[2048,13312]{1,0:T(8,128)(2,1)} %bitcast.134), kind=kOutput, calls=%fused_computation.9 | convolution fusion | flops 13958643712 | bytes 63438848 | tf_op jit(solution)/shard_map/dot_general | solution.py:47
  1740.3 33.9 %reduce-scatter.13.cloned.1.call-done = f32[512,256]{0,1:T(8,128)} async-done(((f32[2048,256]{0,1:T(8,128)}), f32[512,256]{0,1:T(8,128)}) %reduce-scatter.13.cloned.1.call-update) | async-done | bytes 524304 | tf_op jit(solution)/shard_map/reduce_scatter | solution.py:46
  1774.2 1.8 convert_element_type.18
  1776.0 27.0 %all-gather.16.cloned.1.call-done = bf16[2048,256]{0,1:T(8,128)(2,1)} async-done(((bf16[512,256]{0,1:T(8,128)(2,1)}), bf16[2048,256]{0,1:T(8,128)(2,1)}) %all-gather.16.cloned.1.call-update) | async-done | bytes 1048592 | tf_op jit(solution)/shard_map/all_gather | solution.py:36
  1803.0 28.3 %convolution_bitcast_fusion = f32[13312,256]{0,1:T(8,128)} fusion(bf16[2048,256]{0,1:T(8,128)(2,1)} %all-gather.16.cloned.1.call-done, bf16[2048,13312]{1,0:T(8,128)(2,1)} %bitcast.135), kind=kOutput, calls=%fused_computation.6 | convolution fusion | flops 13958643712 | bytes 69206016 | tf_op jit(solution)/shard_map/dot_general | solution.py:37
  1831.6 139.0 %reduce-scatter.15.cloned.1.call-done = f32[1664,256]{0,1:T(8,128)} async-done(((f32[13312,256]{0,1:T(8,128)}), f32[1664,256]{0,1:T(8,128)}) %reduce-scatter.15.cloned.1.call-update) | async-done | bytes 1703952 | tf_op jit(solution)/shard_map/reduce_scatter | solution.py:40
  1970.5 4.7 fusion.40
  1975.3 126.4 %all-reduce.9.cloned.1.call-done = f32[256,256]{0,1:T(8,128)} async-done(((f32[256,256]{0,1:T(8,128)}), f32[256,256]{0,1:T(8,128)}) %all-reduce.9.cloned.1.call-update) | async-done | bytes 262160 | tf_op jit(solution)/shard_map/psum | solution.py:19
  2101.7 1.1 copy.18
  2102.8 1.0 fusion.8
  2103.8 11.7 cholesky.240
  2115.5 9.8 custom-call.19
  2125.8 11.7 cholesky.257
  2140.2 4.2 while.8
  2141.0 1.4 bitcast_dynamic-update-slice_fusion.8
  2143.0 1.4 bitcast_dynamic-update-slice_fusion.8
  2144.4 19.7 custom-call.20
  2166.8 1.0 fusion.1
  2167.9 1.3 fusion
  2169.3 66.8 %all-gather.18.cloned.1.call-done = bf16[13312,256]{0,1:T(8,128)(2,1)} async-done(((bf16[1664,256]{0,1:T(8,128)(2,1)}), bf16[13312,256]{0,1:T(8,128)(2,1)}) %all-gather.18.cloned.1.call-update) | async-done | bytes 6815760 | tf_op jit(solution)/shard_map/all_gather | solution.py:45
  2236.1 25.5 %convolution_bitcast_fusion.2 = f32[2048,256]{0,1:T(8,128)} fusion(bf16[13312,256]{0,1:T(8,128)(2,1)} %all-gather.18.cloned.1.call-done, bf16[2048,13312]{1,0:T(8,128)(2,1)} %bitcast.136), kind=kOutput, calls=%fused_computation.8 | convolution fusion | flops 13958643712 | bytes 63438848 | tf_op jit(solution)/shard_map/dot_general | solution.py:47
  2261.7 49.8 %all-gather.20.cloned.1.call-done = f32[6656,256]{0,1:T(8,128)} async-done(((f32[1664,256]{0,1:T(8,128)}), f32[6656,256]{0,1:T(8,128)}) %all-gather.20.cloned.1.call-update) | async-done | bytes 6815760 | tf_op jit(solution)/shard_map/all_gather | solution.py:54
  2311.4 8.1 copy.20
  2319.5 30.0 %reduce-scatter.17.cloned.1.call-done = f32[512,256]{0,1:T(8,128)} async-done(((f32[2048,256]{0,1:T(8,128)}), f32[512,256]{0,1:T(8,128)}) %reduce-scatter.17.cloned.1.call-update) | async-done | bytes 524304 | tf_op jit(solution)/shard_map/reduce_scatter | solution.py:46
  2349.4 2.0 copy.19
  (91 shorter events, 19.4 us)
Async XLA Ops:
  117.0 608.8 %all-to-all-start = ((bf16[512,8,4,1664]{3,1,0,2:T(8,128)(2,1)}), bf16[512,8,4,1664]{3,1,0,2:T(8,128)(2,1)}, u32[]{:S(2)}, u32[]{:S(2)}) async-start(bf16[512,8,4,1664]{3,1,0,2:T(8,128)(2,1)} %copy.12), calls=%async_computation | async-start | bytes 109051904 | tf_op jit(solution)/shard_map/all_to_all | solution.py:32
  129.0 633.4 %all-gather.8.cloned.1.call-start = ((), (), s32[]{:S(2)}) async-start(), calls=%async_computation.7 | async-start | bytes 1310720 | tf_op jit(solution)/shard_map/all_gather | solution.py:36
  129.8 800.4 %reduce-scatter.7.cloned.1.call-start = ((), (), s32[]{:S(2)}) async-start(), calls=%async_computation.8 | async-start | bytes 15335424 | tf_op jit(solution)/shard_map/reduce_scatter | solution.py:40
  790.6 270.7 %all-reduce.5.cloned.1.call-start = ((), (), s32[]{:S(2)}) async-start(), calls=%async_computation.9 | async-start | bytes 524288 | tf_op jit(solution)/shard_map/psum | solution.py:19
  936.1 187.1 %copy-start = (f32[1664,256]{1,0:T(8,128)S(1)}, f32[1664,256]{1,0:T(8,128)}, u32[]{:S(2)}) copy-start(f32[1664,256]{1,0:T(8,128)} %reduce-scatter.7.cloned.1.call-done) | copy-start | bytes 5111812
  936.1 259.7 %all-gather.10.cloned.1.call-start = ((), (), s32[]{:S(2)}) async-start(), calls=%async_computation.10 | async-start | bytes 7667712 | tf_op jit(solution)/shard_map/all_gather | solution.py:45
  1127.6 126.4 %reduce-scatter.9.cloned.1.call-start = ((), (), s32[]{:S(2)}) async-start(), calls=%async_computation.11 | async-start | bytes 2621440 | tf_op jit(solution)/shard_map/reduce_scatter | solution.py:46
  1220.1 62.6 %all-gather.12.cloned.1.call-start = ((), (), s32[]{:S(2)}) async-start(), calls=%async_computation.12 | async-start | bytes 1310720 | tf_op jit(solution)/shard_map/all_gather | solution.py:36
  1255.9 194.4 %reduce-scatter.11.cloned.1.call-start = ((), (), s32[]{:S(2)}) async-start(), calls=%async_computation.13 | async-start | bytes 15335424 | tf_op jit(solution)/shard_map/reduce_scatter | solution.py:40
  1311.1 270.3 %all-reduce.7.cloned.1.call-start = ((), (), s32[]{:S(2)}) async-start(), calls=%async_computation.14 | async-start | bytes 524288 | tf_op jit(solution)/shard_map/psum | solution.py:19
  1455.0 189.1 %copy-start.2 = (f32[1664,256]{0,1:T(8,128)S(1)}, f32[1664,256]{0,1:T(8,128)}, u32[]{:S(2)}) copy-start(f32[1664,256]{0,1:T(8,128)} %reduce-scatter.11.cloned.1.call-done) | copy-start | bytes 5111812
  1455.0 261.0 %all-gather.14.cloned.1.call-start = ((), (), s32[]{:S(2)}) async-start(), calls=%async_computation.15 | async-start | bytes 7667712 | tf_op jit(solution)/shard_map/all_gather | solution.py:45
  1647.8 126.4 %reduce-scatter.13.cloned.1.call-start = ((), (), s32[]{:S(2)}) async-start(), calls=%async_computation.16 | async-start | bytes 2621440 | tf_op jit(solution)/shard_map/reduce_scatter | solution.py:46
  1740.3 62.7 %all-gather.16.cloned.1.call-start = ((), (), s32[]{:S(2)}) async-start(), calls=%async_computation.17 | async-start | bytes 1310720 | tf_op jit(solution)/shard_map/all_gather | solution.py:36
  1776.0 194.6 %reduce-scatter.15.cloned.1.call-start = ((), (), s32[]{:S(2)}) async-start(), calls=%async_computation.18 | async-start | bytes 15335424 | tf_op jit(solution)/shard_map/reduce_scatter | solution.py:40
  1831.4 270.3 %all-reduce.9.cloned.1.call-start = ((), (), s32[]{:S(2)}) async-start(), calls=%async_computation.19 | async-start | bytes 524288 | tf_op jit(solution)/shard_map/psum | solution.py:19
  1975.2 188.9 %copy-start.1 = (f32[1664,256]{0,1:T(8,128)S(1)}, f32[1664,256]{0,1:T(8,128)}, u32[]{:S(2)}) copy-start(f32[1664,256]{0,1:T(8,128)} %reduce-scatter.15.cloned.1.call-done) | copy-start | bytes 5111812
  1975.2 260.9 %all-gather.18.cloned.1.call-start = ((), (), s32[]{:S(2)}) async-start(), calls=%async_computation.20 | async-start | bytes 7667712 | tf_op jit(solution)/shard_map/all_gather | solution.py:45
  2167.9 143.5 %all-gather.20.cloned.1.call-start = ((), (), s32[]{:S(2)}) async-start(), calls=%async_computation.22 | async-start | bytes 8519680 | tf_op jit(solution)/shard_map/all_gather | solution.py:54
  2169.3 180.2 %reduce-scatter.17.cloned.1.call-start = ((), (), s32[]{:S(2)}) async-start(), calls=%async_computation.21 | async-start | bytes 2621440 | tf_op jit(solution)/shard_map/reduce_scatter | solution.py:46
Sparse Core Ops, SparseCore 0:
  131.7 318.6 all-gather.7
  790.8 139.4 reduce-scatter.6
  936.3 124.9 all-reduce.4
  1127.7 68.0 all-gather.9
  1220.2 33.7 reduce-scatter.8
  1256.3 26.3 all-gather.11
  1311.2 139.0 reduce-scatter.10
  1456.3 125.0 all-reduce.6
  1647.9 68.0 all-gather.13
  1740.4 33.7 reduce-scatter.12
  1776.6 26.3 all-gather.15
  1831.5 139.0 reduce-scatter.14
  1976.6 125.0 all-reduce.8
  2168.0 68.0 all-gather.17
  2238.4 72.9 all-gather.19
  2314.2 35.1 reduce-scatter.16
where the time goes:
time: 2370 us; the launch traced here: 2360 us
  waiting for transfers between devices  1800 us (76%)
  matrix products  184 us (8%)
  other arithmetic  173 us (7%)
  local copies, waits for them, and re-layouts  172 us (7%)
    all_to_all x1, waiting for transfers between devices, shards(): lax.all_to_all(split, 'grad', split_axis=2, concat_axis=0, tiled=True)  596 us
    reduce_scatter x3, waiting for transfers between devices, sketch_of(): return lax.psum_scatter(partial, 'col', scatter_dimension=0, tiled=True)  417 us
    psum x3, waiting for transfers between devices, orthonormal(): gram = lax.psum(partial_gram, ('grad', 'col'))  377 us
    all_gather x3, waiting for transfers between devices, shards(): lax.all_gather(basis_rows.astype(jnp.bfloat16), 'col', axis=0, tiled=True)  203 us
    reshape x2, local copies, waits for them, and re-layouts, shards(): split = gradient.reshape(n_rows, n_col, n_grad, piece)  110 us
    another operation x20, other arithmetic, orthonormal(): lower_factor = jnp.linalg.cholesky(gram)  103 us
    reduce_scatter x3, waiting for transfers between devices, shards(): lax.psum_scatter(jnp.dot(blocks, basis_bf, preferred_element_type=jnp.flo...  97.7 us
    dot_general x3, matrix products, sketch_of(): lax.dot_general(blocks, rows, (((0,), (0,)), ((), ())), preferred_element...  84.8 us
  transfers between devices with their start and end apart: 17, of which 16 were waited for; matrix products, arithmetic and copies ran while one was open for 3% of the time, Pallas kernels for 0%

commit v1 on v0

--- a/solution.py
+++ b/solution.py
@@ -6,6 +6,28 @@
 
 FF = 53248
 POWER = 2
+
+
+def laid_out(blocks, dim):
+    blocks = jnp.moveaxis(blocks, 0, dim)
+    shape = blocks.shape
+    return blocks.reshape(*shape[:dim], shape[dim] * shape[dim + 1], *shape[dim + 2 :])
+
+
+def collect(x, axis, dim):
+    length = lax.axis_size(axis)
+    pairs = [(i, (i + 1) % length) for i in range(length)]
+    back = [(b, a) for a, b in pairs]
+    lower, upper = ([], [])
+    for step in range(length - 1):
+        if step % 2 == 0:
+            lower.append(lax.ppermute(lower[-1] if lower else x, axis, pairs))
+        else:
+            upper.append(lax.ppermute(upper[-1] if upper else x, axis, back))
+    tiles = jnp.stack([*lower[::-1], x, *upper])
+    shift = lax.axis_index(axis) - len(lower)
+    tiles = tiles[(jnp.arange(length) - shift) % length]
+    return laid_out(tiles, dim)
 
 
 def orthonormal(rows):
@@ -51,7 +73,7 @@
         )
         if iteration < POWER:
             sketch = sketch_of(reduced.astype(jnp.bfloat16))
-    projector = lax.all_gather(basis_rows * math.sqrt(FF), "grad", axis=0, tiled=True)
+    projector = collect(basis_rows * math.sqrt(FF), "grad", 0)
     return (reduced, projector)
 
 

time: 2370 us -> 2430 us (1.025)
  waiting for transfers between devices: 1800 us -> 1850 us
    ppermute x0 -> x3, waiting for transfers between devices: none -> 127 us  [the longest x2 91 us: collect(): lower.append(lax.ppermute(lower[-1] if lower else x, axis, pairs))]
    all_gather x1 -> x0, waiting for transfers between devices: 49.8 us -> none  [shards(): lax.all_gather(basis_rows * math.sqrt(FF), 'grad', axis=0, tiled=True)]
    reduce_scatter x3, waiting for transfers between devices: 97.7 us -> 67.8 us  [shards(): lax.psum_scatter(jnp.dot(blocks, basis_bf, preferred_element_type=jnp.flo...]
  transfers between devices with their start and end apart: 17 -> 19, of which waited for: 16 -> 17; matrix products, arithmetic and copies ran while one was open for 3% -> 2% of each run, Pallas kernels for 0% -> 0%
where the time goes in v1:
time: 2430 us; the launch traced here: 2420 us
  waiting for transfers between devices  1850 us (76%)
  matrix products  184 us (8%)
  local copies, waits for them, and re-layouts  178 us (7%)
  other arithmetic  178 us (7%)
    all_to_all x1, waiting for transfers between devices, shards(): lax.all_to_all(split, 'grad', split_axis=2, concat_axis=0, tiled=True)  596 us
    reduce_scatter x3, waiting for transfers between devices, sketch_of(): return lax.psum_scatter(partial, 'col', scatter_dimension=0, tiled=True)  417 us
    psum x3, waiting for transfers between devices, orthonormal(): gram = lax.psum(partial_gram, ('grad', 'col'))  378 us
    all_gather x3, waiting for transfers between devices, shards(): lax.all_gather(basis_rows.astype(jnp.bfloat16), 'col', axis=0, tiled=True)  205 us
    reshape x2, local copies, waits for them, and re-layouts, shards(): split = gradient.reshape(n_rows, n_col, n_grad, piece)  110 us
    another operation x20, other arithmetic, orthonormal(): lower_factor = jnp.linalg.cholesky(gram)  103 us
    ppermute x2, waiting for transfers between devices, collect(): lower.append(lax.ppermute(lower[-1] if lower else x, axis, pairs))  91 us
    dot_general x3, matrix products, sketch_of(): lax.dot_general(blocks, rows, (((0,), (0,)), ((), ())), preferred_element...  84.8 us
  transfers between devices with their start and end apart: 19, of which 17 were waited for; matrix products, arithmetic and copies ran while one was open for 2% of the time, Pallas kernels for 0%

profile of v1, /device:TPU:0, one launch (start us, length us, event | category | flops | bytes accessed | tf_op | source)
XLA Modules:
  0.0 2421.7 jit_solution(8030043300093659749)
XLA Ops:
  7.2 73.2 %reshape.80 = bf16[512,8,4,1664]{3,2,1,0:T(4,128)(2,1)} reshape(bf16[512,53248]{1,0:T(8,128)(2,1)} %param.5) | data formatting | bytes 109051904 | tf_op jit(solution)/shard_map/reshape | solution.py:53
  80.4 36.6 %copy.11 = bf16[512,8,4,1664]{3,1,0,2:T(8,128)(2,1)} copy(bf16[512,8,4,1664]{3,2,1,0:T(4,128)(2,1)} %reshape.80) | data formatting | bytes 109051904 | tf_op jit(solution)/shard_map/reshape | solution.py:53
  117.0 12.1 all-to-all-start
  129.8 596.0 %all-to-all-done = bf16[512,8,4,1664]{3,1,0,2:T(8,128)(2,1)} async-done(((bf16[512,8,4,1664]{3,1,0,2:T(8,128)(2,1)}), bf16[512,8,4,1664]{3,1,0,2:T(8,128)(2,1)}, u32[]{:S(2)}, u32[]{:S(2)}) %all-to-all-start) | async-done | bytes 54525984 | tf_op jit(solution)/shard_map/all_to_all | solution.py:54
  725.8 36.6 %copy.23 = bf16[256,8,8,1664]{3,1,2,0:T(8,128)(2,1)} copy(bf16[256,8,8,1664]{3,2,1,0:T(8,128)(2,1)} %bitcast.43) | data formatting | bytes 109051904
  762.4 28.3 %fusion.40 = f32[13312,256]{1,0:T(8,128)} fusion(bf16[2048,13312]{1,0:T(8,128)(2,1)} %bitcast.139, bf16[2048,256]{1,0:T(8,128)(2,1)} %all-gather.7.cloned.1.call-done), kind=kOutput, calls=%fused_computation.100 | convolution fusion | flops 13958643712 | bytes 69206016 | tf_op jit(solution)/shard_map/dot_general | solution.py:59
  790.8 139.5 %reduce-scatter.7.cloned.1.call-done = f32[1664,256]{1,0:T(8,128)} async-done(((f32[13312,256]{1,0:T(8,128)}), f32[1664,256]{1,0:T(8,128)}) %reduce-scatter.7.cloned.1.call-update) | async-done | bytes 1703952 | tf_op jit(solution)/shard_map/reduce_scatter | solution.py:62
  930.3 5.8 fusion.41
  936.6 124.8 %all-reduce.5.cloned.1.call-done = f32[256,256]{0,1:T(8,128)} async-done(((f32[256,256]{0,1:T(8,128)}), f32[256,256]{0,1:T(8,128)}) %all-reduce.5.cloned.1.call-update) | async-done | bytes 262160 | tf_op jit(solution)/shard_map/psum | solution.py:41
  1061.4 1.1 copy.13
  1063.5 11.7 cholesky.172
  1075.2 9.8 custom-call.15
  1085.6 11.7 cholesky.189
  1099.5 4.2 while.6
  1100.2 1.4 bitcast_dynamic-update-slice_fusion.6
  1102.3 1.4 bitcast_dynamic-update-slice_fusion.6
  1103.7 19.7 custom-call.16
  1124.4 1.5 convolution_subtract_fusion.2
  1127.9 68.2 %all-gather.9.cloned.1.call-done = bf16[13312,256]{0,1:T(8,128)(2,1)} async-done(((bf16[1664,256]{0,1:T(8,128)(2,1)}), bf16[13312,256]{0,1:T(8,128)(2,1)}) %all-gather.9.cloned.1.call-update) | async-done | bytes 6815760 | tf_op jit(solution)/shard_map/all_gather | solution.py:67
  1196.1 24.6 %convolution_bitcast_fusion.4 = f32[2048,256]{0,1:T(8,128)} fusion(bf16[13312,256]{0,1:T(8,128)(2,1)} %all-gather.9.cloned.1.call-done, bf16[2048,13312]{1,0:T(8,128)(2,1)} %bitcast.140), kind=kOutput, calls=%fused_computation.12 | convolution fusion | flops 13958643712 | bytes 63438848 | tf_op jit(solution)/shard_map/dot_general | solution.py:69
  1220.7 33.9 %reduce-scatter.9.cloned.1.call-done = f32[512,256]{0,1:T(8,128)} async-done(((f32[2048,256]{0,1:T(8,128)}), f32[512,256]{0,1:T(8,128)}) %reduce-scatter.9.cloned.1.call-update) | async-done | bytes 524304 | tf_op jit(solution)/shard_map/reduce_scatter | solution.py:68
  1254.6 1.8 convert_element_type.16
  1256.5 26.8 %all-gather.11.cloned.1.call-done = bf16[2048,256]{0,1:T(8,128)(2,1)} async-done(((bf16[512,256]{0,1:T(8,128)(2,1)}), bf16[2048,256]{0,1:T(8,128)(2,1)}) %all-gather.11.cloned.1.call-update) | async-done | bytes 1048592 | tf_op jit(solution)/shard_map/all_gather | solution.py:58
  1283.3 28.3 %convolution_bitcast_fusion.1 = f32[13312,256]{0,1:T(8,128)} fusion(bf16[2048,256]{0,1:T(8,128)(2,1)} %all-gather.11.cloned.1.call-done, bf16[2048,13312]{1,0:T(8,128)(2,1)} %bitcast.141), kind=kOutput, calls=%fused_computation.8 | convolution fusion | flops 13958643712 | bytes 69206016 | tf_op jit(solution)/shard_map/dot_general | solution.py:59
  1311.9 138.9 %reduce-scatter.11.cloned.1.call-done = f32[1664,256]{0,1:T(8,128)} async-done(((f32[13312,256]{0,1:T(8,128)}), f32[1664,256]{0,1:T(8,128)}) %reduce-scatter.11.cloned.1.call-update) | async-done | bytes 1703952 | tf_op jit(solution)/shard_map/reduce_scatter | solution.py:62
  1450.8 4.6 fusion.42
  1455.4 126.5 %all-reduce.7.cloned.1.call-done = f32[256,256]{0,1:T(8,128)} async-done(((f32[256,256]{0,1:T(8,128)}), f32[256,256]{0,1:T(8,128)}) %all-reduce.7.cloned.1.call-update) | async-done | bytes 262160 | tf_op jit(solution)/shard_map/psum | solution.py:41
  1581.9 1.1 copy.15
  1584.0 11.7 cholesky.206
  1595.8 9.8 custom-call.17
  1606.1 11.7 cholesky.223
  1620.5 4.5 while.7
  1621.6 1.4 bitcast_dynamic-update-slice_fusion.7
  1623.6 1.4 bitcast_dynamic-update-slice_fusion.7
  1625.0 19.7 custom-call.18
  1648.5 68.2 %all-gather.13.cloned.1.call-done = bf16[13312,256]{0,1:T(8,128)(2,1)} async-done(((bf16[1664,256]{0,1:T(8,128)(2,1)}), bf16[13312,256]{0,1:T(8,128)(2,1)}) %all-gather.13.cloned.1.call-update) | async-done | bytes 6815760 | tf_op jit(solution)/shard_map/all_gather | solution.py:67
  1716.6 24.6 %convolution_bitcast_fusion.3 = f32[2048,256]{0,1:T(8,128)} fusion(bf16[13312,256]{0,1:T(8,128)(2,1)} %all-gather.13.cloned.1.call-done, bf16[2048,13312]{1,0:T(8,128)(2,1)} %bitcast.142), kind=kOutput, calls=%fused_computation.11 | convolution fusion | flops 13958643712 | bytes 63438848 | tf_op jit(solution)/shard_map/dot_general | solution.py:69
  1741.3 33.9 %reduce-scatter.13.cloned.1.call-done = f32[512,256]{0,1:T(8,128)} async-done(((f32[2048,256]{0,1:T(8,128)}), f32[512,256]{0,1:T(8,128)}) %reduce-scatter.13.cloned.1.call-update) | async-done | bytes 524304 | tf_op jit(solution)/shard_map/reduce_scatter | solution.py:68
  1775.2 1.8 convert_element_type.18
  1777.0 27.0 %all-gather.15.cloned.1.call-done = bf16[2048,256]{0,1:T(8,128)(2,1)} async-done(((bf16[512,256]{0,1:T(8,128)(2,1)}), bf16[2048,256]{0,1:T(8,128)(2,1)}) %all-gather.15.cloned.1.call-update) | async-done | bytes 1048592 | tf_op jit(solution)/shard_map/all_gather | solution.py:58
  1804.0 28.3 %convolution_bitcast_fusion = f32[13312,256]{0,1:T(8,128)} fusion(bf16[2048,256]{0,1:T(8,128)(2,1)} %all-gather.15.cloned.1.call-done, bf16[2048,13312]{1,0:T(8,128)(2,1)} %bitcast.143), kind=kOutput, calls=%fused_computation.7 | convolution fusion | flops 13958643712 | bytes 69206016 | tf_op jit(solution)/shard_map/dot_general | solution.py:59
  1832.5 139.0 %reduce-scatter.15.cloned.1.call-done = f32[1664,256]{0,1:T(8,128)} async-done(((f32[13312,256]{0,1:T(8,128)}), f32[1664,256]{0,1:T(8,128)}) %reduce-scatter.15.cloned.1.call-update) | async-done | bytes 1703952 | tf_op jit(solution)/shard_map/reduce_scatter | solution.py:62
  1971.5 4.6 fusion.43
  1976.2 126.4 %all-reduce.9.cloned.1.call-done = f32[256,256]{0,1:T(8,128)} async-done(((f32[256,256]{0,1:T(8,128)}), f32[256,256]{0,1:T(8,128)}) %all-reduce.9.cloned.1.call-update) | async-done | bytes 262160 | tf_op jit(solution)/shard_map/psum | solution.py:41
  2102.6 1.1 copy.17
  2104.7 11.7 cholesky.240
  2116.5 9.8 custom-call.19
  2126.8 11.7 cholesky.257
  2141.1 4.2 while.8
  2142.0 1.4 bitcast_dynamic-update-slice_fusion.8
  2144.0 1.4 bitcast_dynamic-update-slice_fusion.8
  2145.4 19.7 custom-call.20
  2168.8 68.2 %all-gather.17.cloned.1.call-done = bf16[13312,256]{0,1:T(8,128)(2,1)} async-done(((bf16[1664,256]{0,1:T(8,128)(2,1)}), bf16[13312,256]{0,1:T(8,128)(2,1)}) %all-gather.17.cloned.1.call-update) | async-done | bytes 6815760 | tf_op jit(solution)/shard_map/all_gather | solution.py:67
  2237.0 24.6 %convolution_bitcast_fusion.2 = f32[2048,256]{0,1:T(8,128)} fusion(bf16[13312,256]{0,1:T(8,128)(2,1)} %all-gather.17.cloned.1.call-done, bf16[2048,13312]{1,0:T(8,128)(2,1)} %bitcast.144), kind=kOutput, calls=%fused_computation.10 | convolution fusion | flops 13958643712 | bytes 63438848 | tf_op jit(solution)/shard_map/dot_general | solution.py:69
  2261.6 2.0 fusion.36
  2263.6 1.5 collective-permute-start
  2265.1 1.5 collective-permute-start.2
  2266.6 55.1 %collective-permute-done = f32[1664,256]{0,1:T(8,128)S(1)} collective-permute-done((f32[1664,256]{0,1:T(8,128)}, f32[1664,256]{0,1:T(8,128)S(1)}, u32[]{:S(2)}, u32[]{:S(2)}) %collective-permute-start) | collective-permute-done | bytes 1703968 | tf_op jit(solution)/shard_map/ppermute | solution.py:24
  2322.3 35.9 %collective-permute-done.2 = f32[1664,256]{0,1:T(8,128)S(1)} collective-permute-done((f32[1664,256]{0,1:T(8,128)}, f32[1664,256]{0,1:T(8,128)S(1)}, u32[]{:S(2)}, u32[]{:S(2)}) %collective-permute-start.2) | collective-permute-done | bytes 1703968 | tf_op jit(solution)/shard_map/ppermute | solution.py:26
  2358.2 35.9 %collective-permute-done.1 = f32[1664,256]{0,1:T(8,128)} collective-permute-done((f32[1664,256]{0,1:T(8,128)S(1)}, f32[1664,256]{0,1:T(8,128)}, u32[]{:S(2)}, u32[]{:S(2)}) %collective-permute-start.1) | collective-permute-done | bytes 1703968 | tf_op jit(solution)/shard_map/ppermute | solution.py:24
  2394.1 4.5 pad_maximum_fusion
  2398.6 6.7 gather_fusion
  2405.3 7.6 copy.18
  2412.9 2.0 copy.19
  (98 shorter events, 25.0 us)
Async XLA Ops:
  117.0 608.8 %all-to-all-start = ((bf16[512,8,4,1664]{3,1,0,2:T(8,128)(2,1)}), bf16[512,8,4,1664]{3,1,0,2:T(8,128)(2,1)}, u32[]{:S(2)}, u32[]{:S(2)}) async-start(bf16[512,8,4,1664]{3,1,0,2:T(8,128)(2,1)} %copy.11), calls=%async_computation | async-start | bytes 109051904 | tf_op jit(solution)/shard_map/all_to_all | solution.py:54
  129.0 633.4 %all-gather.7.cloned.1.call-start = ((), (), s32[]{:S(2)}) async-start(), calls=%async_computation.7 | async-start | bytes 1310720 | tf_op jit(solution)/shard_map/all_gather | solution.py:58
  129.8 800.5 %reduce-scatter.7.cloned.1.call-start = ((), (), s32[]{:S(2)}) async-start(), calls=%async_computation.8 | async-start | bytes 15335424 | tf_op jit(solution)/shard_map/reduce_scatter | solution.py:62
  790.7 270.7 %all-reduce.5.cloned.1.call-start = ((), (), s32[]{:S(2)}) async-start(), calls=%async_computation.9 | async-start | bytes 524288 | tf_op jit(solution)/shard_map/psum | solution.py:41
  936.1 187.3 %copy-start = (f32[1664,256]{1,0:T(8,128)S(1)}, f32[1664,256]{1,0:T(8,128)}, u32[]{:S(2)}) copy-start(f32[1664,256]{1,0:T(8,128)} %reduce-scatter.7.cloned.1.call-done) | copy-start | bytes 5111812
  936.1 260.0 %all-gather.9.cloned.1.call-start = ((), (), s32[]{:S(2)}) async-start(), calls=%async_computation.10 | async-start | bytes 7667712 | tf_op jit(solution)/shard_map/all_gather | solution.py:67
  1127.9 126.8 %reduce-scatter.9.cloned.1.call-start = ((), (), s32[]{:S(2)}) async-start(), calls=%async_computation.11 | async-start | bytes 2621440 | tf_op jit(solution)/shard_map/reduce_scatter | solution.py:68
  1220.7 62.6 %all-gather.11.cloned.1.call-start = ((), (), s32[]{:S(2)}) async-start(), calls=%async_computation.12 | async-start | bytes 1310720 | tf_op jit(solution)/shard_map/all_gather | solution.py:58
  1256.4 194.4 %reduce-scatter.11.cloned.1.call-start = ((), (), s32[]{:S(2)}) async-start(), calls=%async_computation.13 | async-start | bytes 15335424 | tf_op jit(solution)/shard_map/reduce_scatter | solution.py:62
  1311.6 270.3 %all-reduce.7.cloned.1.call-start = ((), (), s32[]{:S(2)}) async-start(), calls=%async_computation.14 | async-start | bytes 524288 | tf_op jit(solution)/shard_map/psum | solution.py:41
  1455.4 189.3 %copy-start.2 = (f32[1664,256]{0,1:T(8,128)S(1)}, f32[1664,256]{0,1:T(8,128)}, u32[]{:S(2)}) copy-start(f32[1664,256]{0,1:T(8,128)} %reduce-scatter.11.cloned.1.call-done) | copy-start | bytes 5111812
  1455.4 261.2 %all-gather.13.cloned.1.call-start = ((), (), s32[]{:S(2)}) async-start(), calls=%async_computation.15 | async-start | bytes 7667712 | tf_op jit(solution)/shard_map/all_gather | solution.py:67
  1648.4 126.8 %reduce-scatter.13.cloned.1.call-start = ((), (), s32[]{:S(2)}) async-start(), calls=%async_computation.16 | async-start | bytes 2621440 | tf_op jit(solution)/shard_map/reduce_scatter | solution.py:68
  1741.2 62.8 %all-gather.15.cloned.1.call-start = ((), (), s32[]{:S(2)}) async-start(), calls=%async_computation.17 | async-start | bytes 1310720 | tf_op jit(solution)/shard_map/all_gather | solution.py:58
  1777.0 194.5 %reduce-scatter.15.cloned.1.call-start = ((), (), s32[]{:S(2)}) async-start(), calls=%async_computation.18 | async-start | bytes 15335424 | tf_op jit(solution)/shard_map/reduce_scatter | solution.py:62
  1832.3 270.3 %all-reduce.9.cloned.1.call-start = ((), (), s32[]{:S(2)}) async-start(), calls=%async_computation.19 | async-start | bytes 524288 | tf_op jit(solution)/shard_map/psum | solution.py:41
  1976.1 189.0 %copy-start.1 = (f32[1664,256]{0,1:T(8,128)S(1)}, f32[1664,256]{0,1:T(8,128)}, u32[]{:S(2)}) copy-start(f32[1664,256]{0,1:T(8,128)} %reduce-scatter.15.cloned.1.call-done) | copy-start | bytes 5111812
  1976.1 260.9 %all-gather.17.cloned.1.call-start = ((), (), s32[]{:S(2)}) async-start(), calls=%async_computation.20 | async-start | bytes 7667712 | tf_op jit(solution)/shard_map/all_gather | solution.py:67
  2168.8 244.1 %reduce-scatter.17.cloned.1.call-start = ((), (), s32[]{:S(2)}) async-start(), calls=%async_computation.21 | async-start | bytes 2621440 | tf_op jit(solution)/shard_map/reduce_scatter | solution.py:68
  2263.6 58.0 %collective-permute-start = (f32[1664,256]{0,1:T(8,128)}, f32[1664,256]{0,1:T(8,128)S(1)}, u32[]{:S(2)}, u32[]{:S(2)}) collective-permute-start(f32[1664,256]{0,1:T(8,128)} %get-tuple-element.62), channel_id=1, source_target_pairs={{0,8},{8,16},{16,24},{24,0},{1,9},{9,17},{17,25},{25,1},{2,10},{10... | collective-permute-start | bytes 5111816 | tf_op jit(solution)/shard_map/ppermute | solution.py:24
  2265.1 93.1 %collective-permute-start.2 = (f32[1664,256]{0,1:T(8,128)}, f32[1664,256]{0,1:T(8,128)S(1)}, u32[]{:S(2)}, u32[]{:S(2)}) collective-permute-start(f32[1664,256]{0,1:T(8,128)} %get-tuple-element.62), channel_id=1, source_target_pairs={{8,0},{16,8},{24,16},{0,24},{9,1},{17,9},{25,17},{1,25},{10,2},{18... | collective-permute-start | bytes 5111816 | tf_op jit(solution)/shard_map/ppermute | solution.py:26
  2321.7 72.4 %collective-permute-start.1 = (f32[1664,256]{0,1:T(8,128)S(1)}, f32[1664,256]{0,1:T(8,128)}, u32[]{:S(2)}, u32[]{:S(2)}) collective-permute-start(f32[1664,256]{0,1:T(8,128)S(1)} %collective-permute-done), channel_id=1, source_target_pairs={{0,8},{8,16},{16,24},{24,0},{1,9},{9,17},{17,25},{25,1},{2,10},{10... | collective-permute-start | bytes 5111816 | tf_op jit(solution)/shard_map/ppermute | solution.py:24
Sparse Core Ops, SparseCore 0:
  131.7 318.6 all-gather.6
  790.8 139.4 reduce-scatter.6
  936.4 124.9 all-reduce.4
  1128.0 68.0 all-gather.8
  1220.8 33.7 reduce-scatter.8
  1256.9 26.3 all-gather.10
  1311.7 139.0 reduce-scatter.10
  1456.9 125.0 all-reduce.6
  1648.5 68.0 all-gather.12
  1741.4 33.7 reduce-scatter.12
  1777.6 26.3 all-gather.14
  1832.4 139.0 reduce-scatter.14
  1977.6 124.9 all-reduce.8
  2168.9 68.0 all-gather.16
  2261.8 51.7 reduce-scatter.16
